TPU v7x, 32 devices: a whole 2x2x4 slice. The times are simulated.
32 devices in a mesh: group: 2 (over y), seq: 4 (over z), batch: 2 (over x), chan: 2 (over core).
Axes of the slice: x: 2, y: 2, z: 4, core: 2. Of those that a mesh axis runs over, the one named last changes fastest.
Arguments:
- seq_in: bfloat16 [4, 4096, 768], P(('group', 'batch'), 'seq', 'chan'), parts along dimension 0, may hold values from -6 to 6
- conv_weight: bfloat16 [3, 768, 768], P(None, 'chan'), may hold values from -0.125 to 0.125
- cotangent: bfloat16 [4, 2048, 768], P(('group', 'batch'), 'seq', 'chan'), parts along dimension 0, may hold values from -0.59765625 to 0.59765625
Outputs:
- block_out: bfloat16 [4, 2048, 768], P(('group', 'batch'), 'seq', 'chan'), parts along dimension 0
- input_grad: bfloat16 [4, 4096, 768], P(('group', 'batch'), 'seq', 'chan'), parts along dimension 0
- weight_grad: float32 [6, 768, 768], P('group', 'chan', 'batch'), parts along dimension 0
There are 2 independent parts, one for each index of `group`. A program takes and returns all parts, laid end to end along the dimension named above; an argument that names none is the same for every part. Nothing has to cross between parts.
All inputs are finite; a program needn't handle non-finite values.
Results may differ from a plain program's by a relative error of at most 0.0031.
Values may be sent and summed in bfloat16 or wider, within the bound.
No kernel may reach another device: no remote copies, remote signals or barrier semaphores. Data moves between devices by JAX's collectives and lax.ppermute only.
A program may use at most 64 MiB of HBM per device.

v0:
```python
import jax
import jax.numpy as jnp
from jax import lax
from jax.sharding import PartitionSpec as P


def shift_from(block, axis, distance):
    size = lax.axis_size(axis)
    route = [(i - distance, i) for i in range(size) if 0 <= i - distance < size]
    return lax.ppermute(block, axis, route)


def half_of(array, index, axis):
    parts = 2
    shape = array.shape
    split = shape[:axis] + (parts, shape[axis] // parts) + shape[axis + 1 :]
    return lax.dynamic_index_in_dim(array.reshape(split), index, axis, keepdims=False)


def shards(seq_in, conv_weight, cotangent):
    local_in = seq_in[0]
    local_cot = cotangent[0]
    rows = local_in.shape[0] // 2
    width = local_in.shape[1]
    spread = rows // 2
    pooled = 0.5 * jnp.sum(local_in.astype(jnp.float32).reshape(rows, 2, width), axis=1)
    activation = jax.nn.gelu(pooled).astype(jnp.bfloat16)
    both = jnp.stack([activation, local_cot])
    from_prev = shift_from(both[:, rows - spread :], "seq", 1)
    from_next = shift_from(both[:, :spread], "seq", -1)
    own_ext = jnp.concatenate([from_prev, both, from_next], 1)
    full_ext = lax.all_gather(own_ext, "chan", axis=2, tiled=True)
    act_full, cot_full = (full_ext[0], full_ext[1])
    weight_cols = lax.all_to_all(conv_weight, "chan", 2, 1, tiled=True)
    act_taps = jnp.stack([act_full[k * spread : k * spread + rows] for k in range(3)], 1)
    conv_out = jnp.dot(
        act_taps.reshape(rows, -1),
        weight_cols.reshape(-1, weight_cols.shape[2]),
        preferred_element_type=jnp.float32,
    )
    block_out = (pooled + conv_out).astype(jnp.bfloat16)
    cot_taps = jnp.stack(
        [cot_full[(2 - k) * spread : (2 - k) * spread + rows] for k in range(3)], 1
    )
    activ_grad = jnp.einsum(
        "tko,kio->ti", cot_taps, conv_weight, preferred_element_type=jnp.float32
    )
    unused, gelu_back = jax.vjp(jax.nn.gelu, pooled)
    pooled_grad = local_cot.astype(jnp.float32) + gelu_back(activ_grad)[0]
    input_grad = jnp.repeat(0.5 * pooled_grad, 2, axis=0).astype(jnp.bfloat16)
    own_taps = jnp.stack([own_ext[0, k * spread : k * spread + rows] for k in range(3)], 1)
    cot_mid = cot_full[spread : spread + rows]
    batch_count = lax.axis_size("batch")
    if batch_count == 2:
        b = lax.axis_index("batch")
        send = jnp.einsum(
            "tki,to->kio", own_taps, half_of(cot_mid, 1 - b, 1), preferred_element_type=jnp.float32
        )
        keep = jnp.einsum(
            "tki,to->kio", own_taps, half_of(cot_mid, b, 1), preferred_element_type=jnp.float32
        )
        summed = keep + lax.ppermute(send, "batch", [(0, 1), (1, 0)])
    else:
        partial = jnp.einsum("tki,to->kio", own_taps, cot_mid, preferred_element_type=jnp.float32)
        summed = lax.psum_scatter(partial, "batch", scatter_dimension=2, tiled=True)
    weight_grad = lax.psum(summed, "seq")
    return (block_out[None], input_grad[None], weight_grad)


def solution(mesh):
    in_specs = (
        P(("group", "batch"), "seq", "chan"),
        P(None, "chan", None),
        P(("group", "batch"), "seq", "chan"),
    )
    out_specs = (
        P(("group", "batch"), "seq", "chan"),
        P(("group", "batch"), "seq", "chan"),
        P("group", "chan", "batch"),
    )
    return jax.shard_map(shards, mesh=mesh, in_specs=in_specs, out_specs=out_specs, check_vma=False)
```

profile of v0, /device:TPU:0, one launch (start us, length us, event | category | flops | bytes accessed | tf_op | source)
XLA Modules:
  0.0 179.5 jit_solution(5351627847527597983)
XLA Ops:
  7.2 2.2 %reshape.129 = f32[512,2,384]{2,1,0:T(2,128)S(1)} reshape(bf16[1,1024,384]{2,1,0:T(8,128)(2,1)} %param.3) | data formatting | bytes 2359296 | tf_op jit(solution)/shard_map/convert_element_type | solution.py:26
  9.4 1.9 %reduce_sum.9 = f32[512,384]{1,0:T(8,128)S(1)} reduce(f32[512,2,384]{2,1,0:T(2,128)S(1)} %reshape.129, f32[]{:T(128)} %constant.8.clone.1), dimensions={1}, to_apply=%region_0.0 | reduce | flops 196608 | bytes 2359300 | tf_op jit(solution)/shard_map/reduce_sum | solution.py:26
  11.3 0.3 fusion.27
  11.6 0.1 fusion.39
  11.7 5.0 %collective-permute-start = (bf16[2,256,384]{2,1,0:T(8,128)(2,1)S(1)}, bf16[2,256,384]{2,1,0:T(8,128)(2,1)S(1)}, u32[]{:S(2)}, u32[]{:S(2)}) collective-permute-start(bf16[2,256,384]{2,1,0:T(8,128)(2,1)S(1)} %get-tuple-element.14), channel_id=1, source_target_pairs={{0,4},{4,8},{8,12},{1,5},{5,9},{9,13},{2,6},{6,10},{10,14},{3,7},{... | collective-permute-start | bytes 1179656 | tf_op jit(solution)/shard_map/ppermute | solution.py:10
  16.7 1.3 collective-permute-start.1
  18.0 7.0 %collective-permute-done = bf16[2,256,384]{2,1,0:T(8,128)(2,1)S(1)} collective-permute-done((bf16[2,256,384]{2,1,0:T(8,128)(2,1)S(1)}, bf16[2,256,384]{2,1,0:T(8,128)(2,1)S(1)}, u32[]{:S(2)}, u32[]{:S(2)}) %collective-permute-start) | collective-permute-done | bytes 393248 | tf_op jit(solution)/shard_map/ppermute | solution.py:10
  25.0 4.1 %collective-permute-done.1 = bf16[2,256,384]{2,1,0:T(8,128)(2,1)S(1)} collective-permute-done((bf16[2,256,384]{2,1,0:T(8,128)(2,1)S(1)}, bf16[2,256,384]{2,1,0:T(8,128)(2,1)S(1)}, u32[]{:S(2)}, u32[]{:S(2)}) %collective-permute-start.1) | collective-permute-done | bytes 393248 | tf_op jit(solution)/shard_map/ppermute | solution.py:10
  29.1 1.3 pad_maximum_fusion.1
  30.5 0.0 all-reduce.2.cloned.1.call-start
  30.5 1.0 fusion.35
  31.6 0.1 fusion.41
  31.6 11.2 %all-gather.2.cloned.1.call-done = bf16[2,1024,768]{2,1,0:T(8,128)(2,1)} async-done(((bf16[2,1024,384]{2,1,0:T(8,128)(2,1)}), bf16[2,1024,768]{2,1,0:T(8,128)(2,1)}) %all-gather.2.cloned.1.call-update) | async-done | bytes 3145744 | tf_op jit(solution)/shard_map/all_gather | solution.py:32
  42.8 4.6 %fusion.45 = (bf16[1,512,768]{2,1,0:T(8,128)(2,1)S(1)}, bf16[512,1,768]{2,0,1:T(8,128)(2,1)}, bf16[512,1,768]{2,0,1:T(8,128)(2,1)}, bf16[512,1,768]{2,0,1:T(8,12...) fusion(bf16[2,1024,768]{2,1,0:T(8,128)(2,1)} %all-gather.2.cloned.1.call-done), kind=kLoop, calls=%fused_computation.67 | loop fusion | bytes 10223616 | tf_op jit(solution)/shard_map/slice | solution.py:43
  47.4 0.2 reshape.128
  47.6 1.6 constant_dynamic-slice_fusion.1
  49.3 0.8 fusion.38
  50.1 1.8 %collective-permute-start.2 = (f32[3,384,384]{2,1,0:T(8,128)S(1)}, f32[3,384,384]{2,1,0:T(8,128)S(1)}, u32[]{:S(2)}, u32[]{:S(2)}) collective-permute-start(f32[3,384,384]{2,1,0:T(8,128)S(1)} %fusion.38), channel_id=1, source_target_pairs={{0,2},{2,0},{1,3},{3,1},{4,6},{6,4},{5,7},{7,5},{8,10},{10,8},{9,1... | collective-permute-start | bytes 5308424 | tf_op jit(solution)/shard_map/ppermute | solution.py:62
  51.9 39.1 %collective-permute-done.2 = f32[3,384,384]{2,1,0:T(8,128)S(1)} collective-permute-done((f32[3,384,384]{2,1,0:T(8,128)S(1)}, f32[3,384,384]{2,1,0:T(8,128)S(1)}, u32[]{:S(2)}, u32[]{:S(2)}) %collective-permute-start.2) | collective-permute-done | bytes 1769504 | tf_op jit(solution)/shard_map/ppermute | solution.py:62
  91.0 2.0 %convolution_add_fusion = f32[3,384,384]{2,1,0:T(8,128)} fusion(f32[3,384,384]{2,1,0:T(8,128)S(1)} %collective-permute-done.2, bf16[512,1,384]{2,0,1:T(8,128)(2,1)S(1)} %get-tuple-element.13, bf16[512,1,384]{2,0,1:T(8,128)(2,1)S(1)} %copy-done.1, bf16[512,1,384]{2,0,1:T(8,128)(2,1)S(1)} %get-tuple-element.12, bf16[512,1,384]{2,1,0:T(2,128)(2,1)S(1)} %get-tuple-element.10), kind=kOutput, calls=%fused_computation.8 | convolution fusion | flops 454606848 | bytes 5111808 | tf_op jit(solution)/shard_map/tki,to->kio/dot_general | solution.py:59
  93.0 4.0 %copy.21 = bf16[3,384,768]{1,0,2:T(4,128)(2,1)S(1)} copy(bf16[3,384,768]{2,1,0:T(8,128)(2,1)} %param.4) | data formatting | bytes 3538944 | tf_op args[1]
  97.0 5.6 %all_to_all.15 = bf16[3,384,768]{1,0,2:T(4,128)(2,1)S(1)} all-to-all(bf16[3,384,768]{1,0,2:T(4,128)(2,1)S(1)} %copy.21), channel_id=1, replica_groups=mesh['group'=2,'seq'=4,'batch'=2,'chan'=2] {'chan'}, dimensions={2} | all-to-all | bytes 3538944 | tf_op jit(solution)/shard_map/all_to_all | solution.py:34
  102.6 0.2 copy.22
  102.9 2.3 %copy.23 = bf16[3,2,384,384]{3,2,1,0:T(8,128)(2,1)} copy(bf16[3,2,384,384]{2,3,1,0:T(8,128)(2,1)S(1)} %bitcast.46) | data formatting | bytes 3538944 | tf_op jit(solution)/shard_map/all_to_all | solution.py:34
  105.1 4.0 %fusion.19 = bf16[512,384]{1,0:T(8,128)(2,1)S(1)} fusion(bf16[3,384,768]{2,1,0:T(8,128)(2,1)} %param.4, bf16[512,1,768]{2,0,1:T(8,128)(2,1)} %get-tuple-element.5, bf16[512,1,768]{2,0,1:T(8,128)(2,1)} %get-tuple-element.4, bf16[512,1,768]{2,0,1:T(8,128)(2,1)} %get-tuple-element.6, f32[512,384]{1,0:T(8,128)S(1)} %reduce_sum.9, ...), kind=kOutput, calls=%fused_computation.26 | convolution fusion | flops 913047552 | bytes 5701632 | tf_op jit(solution)/shard_map/tko,kio->ti/dot_general | solution.py:45
  109.2 0.4 broadcast_in_dim.8
  109.6 1.2 convert_element_type.60
  110.8 1.9 %pad_maximum_fusion = bf16[512,3,768]{2,0,1:T(8,128)(2,1)S(1)} fusion(bf16[512,1,768]{2,0,1:T(8,128)(2,1)} %get-tuple-element.7, bf16[512,1,768]{2,0,1:T(8,128)(2,1)} %get-tuple-element.8, bf16[512,1,768]{2,0,1:T(8,128)(2,1)} %get-tuple-element.9), kind=kLoop, calls=%fused_computation | loop fusion | flops 2359296 | bytes 4718592 | tf_op jit(solution)/shard_map/stack | solution.py:35
  112.7 2.5 %copy.20 = bf16[512,3,768]{0,2,1:T(8,128)(2,1)} copy(bf16[512,3,768]{2,0,1:T(8,128)(2,1)S(1)} %pad_maximum_fusion) | data formatting | bytes 4718592 | tf_op jit(solution)/shard_map/stack | solution.py:35
  115.2 4.4 %fusion.10 = bf16[1,512,384]{2,1,0:T(8,128)(2,1)} fusion(bf16[512,2304]{0,1:T(8,128)(2,1)} %bitcast.45, bf16[2304,384]{1,0:T(8,128)(2,1)} %bitcast.47, f32[512,384]{1,0:T(8,128)S(1)} %reduce_sum.9), kind=kOutput, calls=%fused_computation.12 | convolution fusion | flops 906559488 | bytes 5308416 | tf_op jit(solution)/shard_map/dot_general | solution.py:36
  119.6 50.3 %all-reduce.2.cloned.1.call-done = f32[3,384,384]{2,1,0:T(8,128)} async-done(((f32[3,384,384]{2,1,0:T(8,128)}), f32[3,384,384]{2,1,0:T(8,128)}) %all-reduce.2.cloned.1.call-update) | async-done | bytes 1769488 | tf_op jit(solution)/shard_map/psum | solution.py:66
  169.8 2.8 %copy.37 = f32[3,384,384]{2,1,0:T(8,128)} copy(f32[3,384,384]{2,1,0:T(8,128)} %all-reduce.2.cloned.1.call-done) | data formatting | bytes 3538944
  (7 shorter events, 0.1 us)
Async XLA Ops:
  7.2 35.7 %all-gather.2.cloned.1.call-start = ((), (), s32[]{:S(2)}) async-start(), calls=%async_computation.1 | async-start | bytes 4718592 | tf_op jit(solution)/shard_map/all_gather | solution.py:32
  9.4 2.2 %copy-start = (bf16[1,512,384]{2,1,0:T(8,128)(2,1)S(1)}, bf16[1,512,384]{2,1,0:T(8,128)(2,1)}, u32[]{:S(2)}) copy-start(bf16[1,512,384]{2,1,0:T(8,128)(2,1)} %param.5) | copy-start | bytes 1179652
  11.7 13.3 %collective-permute-start = (bf16[2,256,384]{2,1,0:T(8,128)(2,1)S(1)}, bf16[2,256,384]{2,1,0:T(8,128)(2,1)S(1)}, u32[]{:S(2)}, u32[]{:S(2)}) collective-permute-start(bf16[2,256,384]{2,1,0:T(8,128)(2,1)S(1)} %get-tuple-element.14), channel_id=1, source_target_pairs={{0,4},{4,8},{8,12},{1,5},{5,9},{9,13},{2,6},{6,10},{10,14},{3,7},{... | collective-permute-start | bytes 1179656 | tf_op jit(solution)/shard_map/ppermute | solution.py:10
  16.7 12.5 %collective-permute-start.1 = (bf16[2,256,384]{2,1,0:T(8,128)(2,1)S(1)}, bf16[2,256,384]{2,1,0:T(8,128)(2,1)S(1)}, u32[]{:S(2)}, u32[]{:S(2)}) collective-permute-start(bf16[2,256,384]{2,1,0:T(8,128)(2,1)S(1)} %get-tuple-element.15), channel_id=1, source_target_pairs={{4,0},{8,4},{12,8},{5,1},{9,5},{13,9},{6,2},{10,6},{14,10},{7,3},{... | collective-permute-start | bytes 1179656 | tf_op jit(solution)/shard_map/ppermute | solution.py:10
  30.5 139.4 %all-reduce.2.cloned.1.call-start = ((), (), s32[]{:S(2)}) async-start(), calls=%async_computation.2 | async-start | bytes 3538944 | tf_op jit(solution)/shard_map/psum | solution.py:66
  47.6 1.6 copy-start.1
  50.1 40.9 %collective-permute-start.2 = (f32[3,384,384]{2,1,0:T(8,128)S(1)}, f32[3,384,384]{2,1,0:T(8,128)S(1)}, u32[]{:S(2)}, u32[]{:S(2)}) collective-permute-start(f32[3,384,384]{2,1,0:T(8,128)S(1)} %fusion.38), channel_id=1, source_target_pairs={{0,2},{2,0},{1,3},{3,1},{4,6},{6,4},{5,7},{7,5},{8,10},{10,8},{9,1... | collective-permute-start | bytes 5308424 | tf_op jit(solution)/shard_map/ppermute | solution.py:62
Sparse Core Ops, SparseCore 0:
  30.6 12.2 all-gather.1
  93.2 76.6 all-reduce.1
where the time goes:
time: 180 us; the launch traced here: 179 us
  waiting for transfers between devices  112 us (62%)
  local copies, waits for them, and re-layouts  21.9 us (12%)
  between operations  14.2 us (8%)
  matrix products  11.3 us (6%)
  starting transfers between devices  8.15 us (5%)
  other arithmetic  6.57 us (4%)
  blocking collectives  5.63 us (3%)
    psum x1, waiting for transfers between devices, shards(): weight_grad = lax.psum(summed, 'seq')  50.3 us
    ppermute x1, waiting for transfers between devices, shards(): summed = keep + lax.ppermute(send, 'batch', [(0, 1), (1, 0)])  39.1 us
    all_gather x1, waiting for transfers between devices, shards(): full_ext = lax.all_gather(own_ext, 'chan', axis=2, tiled=True)  11.2 us
    ppermute x2, waiting for transfers between devices, shift_from(): return lax.ppermute(block, axis, route)  11.2 us
    unnamed x6, local copies, waits for them, and re-layouts  6.76 us
    ppermute x2, starting transfers between devices, shift_from(): return lax.ppermute(block, axis, route)  6.27 us
    all_to_all x1, blocking collectives, shards(): weight_cols = lax.all_to_all(conv_weight, 'chan', 2, 1, tiled=True)  5.63 us
    slice x1, local copies, waits for them, and re-layouts, shards(): cot_full[(2 - k) * spread:(2 - k) * spread + rows]  4.6 us
  transfers between devices with their start and end apart: 5, of which 5 were waited for; matrix products, arithmetic and copies ran while one was open for 12% of the time, Pallas kernels for 0%

commit v1 on v0

--- a/solution.py
+++ b/solution.py
@@ -63,7 +63,7 @@
     else:
         partial = jnp.einsum("tki,to->kio", own_taps, cot_mid, preferred_element_type=jnp.float32)
         summed = lax.psum_scatter(partial, "batch", scatter_dimension=2, tiled=True)
-    weight_grad = lax.psum(summed, "seq")
+    weight_grad = jnp.sum(lax.all_gather(summed, "seq"), axis=0)
     return (block_out[None], input_grad[None], weight_grad)
 
 

time: 180 us -> 235 us (1.31)
  waiting for transfers between devices: 112 us -> 162 us
  other arithmetic: 6.57 us -> 11.5 us
    all_gather x0 -> x1, waiting for transfers between devices: none -> 101 us  [shards(): weight_grad = jnp.sum(lax.all_gather(summed, 'seq'), axis=0)]
    psum x1 -> x0, waiting for transfers between devices: 50.3 us -> none  [shards(): weight_grad = lax.psum(summed, 'seq')]
    reduce_sum x0 -> x1, other arithmetic: none -> 4.78 us  [shards(): weight_grad = jnp.sum(lax.all_gather(summed, 'seq'), axis=0)]
    ppermute x2, waiting for transfers between devices: 11.2 us -> 8.33 us  [shift_from(): return lax.ppermute(block, axis, route)]
    unnamed x6 -> x7, local copies, waits for them, and re-layouts: 6.76 us -> 3.97 us
  transfers between devices with their start and end apart: 5 -> 5, of which waited for: 5 -> 5; matrix products, arithmetic and copies ran while one was open for 12% -> 10% of each run, Pallas kernels for 0% -> 0%
where the time goes in v1:
time: 235 us; the launch traced here: 234 us
  waiting for transfers between devices  162 us (69%)
  local copies, waits for them, and re-layouts  21.9 us (9%)
  between operations  14.2 us (6%)
  other arithmetic  11.5 us (5%)
  matrix products  10.6 us (5%)
  starting transfers between devices  8.78 us (4%)
  blocking collectives  5.63 us (2%)
    all_gather x1, waiting for transfers between devices, shards(): weight_grad = jnp.sum(lax.all_gather(summed, 'seq'), axis=0)  101 us
    ppermute x1, waiting for transfers between devices, shards(): summed = keep + lax.ppermute(send, 'batch', [(0, 1), (1, 0)])  39.1 us
    all_gather x1, waiting for transfers between devices, shards(): full_ext = lax.all_gather(own_ext, 'chan', axis=2, tiled=True)  13.3 us
    ppermute x2, waiting for transfers between devices, shift_from(): return lax.ppermute(block, axis, route)  8.33 us
    ppermute x2, starting transfers between devices, shift_from(): return lax.ppermute(block, axis, route)  6.9 us
    all_to_all x1, blocking collectives, shards(): weight_cols = lax.all_to_all(conv_weight, 'chan', 2, 1, tiled=True)  5.63 us
    reduce_sum x1, other arithmetic, shards(): weight_grad = jnp.sum(lax.all_gather(summed, 'seq'), axis=0)  4.78 us
  transfers between devices with their start and end apart: 5, of which 5 were waited for; matrix products, arithmetic and copies ran while one was open for 10% of the time, Pallas kernels for 0%

profile of v1, /device:TPU:0, one launch (start us, length us, event | category | flops | bytes accessed | tf_op | source)
XLA Modules:
  0.0 234.1 jit_solution(6054210757039204400)
XLA Ops:
  7.2 2.2 reshape.129
  9.4 1.9 reduce_sum.18
  11.3 0.3 fusion.27
  11.6 0.1 fusion.39
  11.7 1.3 collective-permute-start.1
  13.0 5.6 %collective-permute-start = (bf16[2,256,384]{2,1,0:T(8,128)(2,1)S(1)}, bf16[2,256,384]{2,1,0:T(8,128)(2,1)S(1)}, u32[]{:S(2)}, u32[]{:S(2)}) collective-permute-start(bf16[2,256,384]{2,1,0:T(8,128)(2,1)S(1)} %get-tuple-element.14), channel_id=1, source_target_pairs={{0,4},{4,8},{8,12},{1,5},{5,9},{9,13},{2,6},{6,10},{10,14},{3,7},{... | collective-permute-start | bytes 1179656 | tf_op jit(solution)/shard_map/ppermute | solution.py:10
  18.6 7.2 %collective-permute-done.1 = bf16[2,256,384]{2,1,0:T(8,128)(2,1)S(1)} collective-permute-done((bf16[2,256,384]{2,1,0:T(8,128)(2,1)S(1)}, bf16[2,256,384]{2,1,0:T(8,128)(2,1)S(1)}, u32[]{:S(2)}, u32[]{:S(2)}) %collective-permute-start.1) | collective-permute-done | bytes 393248 | tf_op jit(solution)/shard_map/ppermute | solution.py:10
  25.7 1.2 collective-permute-done
  26.9 1.3 pad_maximum_fusion.1
  28.2 0.0 all-gather.6.cloned.1.call-start
  28.3 1.0 fusion.35
  29.3 0.1 fusion.41
  29.4 13.3 %all-gather.4.cloned.1.call-done = bf16[2,1024,768]{2,1,0:T(8,128)(2,1)} async-done(((bf16[2,1024,384]{2,1,0:T(8,128)(2,1)}), bf16[2,1024,768]{2,1,0:T(8,128)(2,1)}) %all-gather.4.cloned.1.call-update) | async-done | bytes 3145744 | tf_op jit(solution)/shard_map/all_gather | solution.py:32
  42.8 4.7 %fusion.45 = (bf16[1,512,768]{2,1,0:T(8,128)(2,1)S(1)}, bf16[512,1,768]{2,0,1:T(8,128)(2,1)}, bf16[512,1,768]{2,0,1:T(8,128)(2,1)}, bf16[512,1,768]{2,0,1:T(8,12...) fusion(bf16[2,1024,768]{2,1,0:T(8,128)(2,1)} %all-gather.4.cloned.1.call-done), kind=kLoop, calls=%fused_computation.67 | loop fusion | bytes 10223616 | tf_op jit(solution)/shard_map/slice | solution.py:43
  47.4 0.2 reshape.128
  47.6 1.6 constant_dynamic-slice_fusion.1
  49.2 0.8 fusion.38
  50.1 1.8 collective-permute-start.2
  51.9 39.1 %collective-permute-done.2 = f32[3,384,384]{2,1,0:T(8,128)S(1)} collective-permute-done((f32[3,384,384]{2,1,0:T(8,128)S(1)}, f32[3,384,384]{2,1,0:T(8,128)S(1)}, u32[]{:S(2)}, u32[]{:S(2)}) %collective-permute-start.2) | collective-permute-done | bytes 1769504 | tf_op jit(solution)/shard_map/ppermute | solution.py:62
  90.9 2.1 convolution_add_fusion
  93.0 4.0 %copy.21 = bf16[3,384,768]{1,0,2:T(4,128)(2,1)S(1)} copy(bf16[3,384,768]{2,1,0:T(8,128)(2,1)} %param.4) | data formatting | bytes 3538944 | tf_op args[1]
  97.0 5.6 %all_to_all.15 = bf16[3,384,768]{1,0,2:T(4,128)(2,1)S(1)} all-to-all(bf16[3,384,768]{1,0,2:T(4,128)(2,1)S(1)} %copy.21), channel_id=1, replica_groups=mesh['group'=2,'seq'=4,'batch'=2,'chan'=2] {'chan'}, dimensions={2} | all-to-all | bytes 3538944 | tf_op jit(solution)/shard_map/all_to_all | solution.py:34
  102.6 0.2 copy.22
  102.8 2.3 copy.23
  105.1 2.1 pad_maximum_fusion
  107.2 2.6 %copy.20 = bf16[512,3,768]{0,2,1:T(8,128)(2,1)} copy(bf16[512,3,768]{2,0,1:T(8,128)(2,1)S(1)} %pad_maximum_fusion) | data formatting | bytes 4718592 | tf_op jit(solution)/shard_map/stack | solution.py:35
  109.7 4.0 %fusion.19 = bf16[512,384]{1,0:T(8,128)(2,1)S(1)} fusion(bf16[3,384,768]{2,1,0:T(8,128)(2,1)} %param.4, bf16[512,1,768]{2,0,1:T(8,128)(2,1)} %get-tuple-element.5, bf16[512,1,768]{2,0,1:T(8,128)(2,1)} %get-tuple-element.4, bf16[512,1,768]{2,0,1:T(8,128)(2,1)} %get-tuple-element.6, f32[512,384]{1,0:T(8,128)S(1)} %reduce_sum.18, ...), kind=kOutput, calls=%fused_computation.26 | convolution fusion | flops 913047552 | bytes 5701632 | tf_op jit(solution)/shard_map/tko,kio->ti/dot_general | solution.py:45
  113.8 1.3 broadcast_in_dim.8
  115.1 3.0 %convert_element_type.60 = bf16[1,1024,384]{2,1,0:T(8,128)(2,1)} reshape(bf16[512,2,384]{2,1,0:T(2,128)(2,1)} %broadcast_in_dim.8) | data formatting | bytes 1572864 | tf_op jit(solution)/shard_map/convert_element_type | solution.py:50
  118.0 3.7 %fusion.10 = bf16[1,512,384]{2,1,0:T(8,128)(2,1)} fusion(bf16[512,2304]{0,1:T(8,128)(2,1)S(1)} %bitcast.46, bf16[2304,384]{1,0:T(8,128)(2,1)} %bitcast.49, f32[512,384]{1,0:T(8,128)S(1)} %reduce_sum.18), kind=kOutput, calls=%fused_computation.12 | convolution fusion | flops 906559488 | bytes 5308416 | tf_op jit(solution)/shard_map/dot_general | solution.py:36
  121.7 100.8 %all-gather.6.cloned.1.call-done = f32[12,384,384]{2,1,0:T(8,128)} async-done(((f32[3,384,384]{2,1,0:T(8,128)}), f32[12,384,384]{2,1,0:T(8,128)}) %all-gather.6.cloned.1.call-update) | async-done | bytes 7077904 | tf_op jit(solution)/shard_map/all_gather | solution.py:66
  222.5 4.8 %reduce_sum.19 = f32[3,384,384]{2,1,0:T(8,128)} reduce(f32[4,3,384,384]{3,2,1,0:T(8,128)} %bitcast.47, f32[]{:T(128)} %constant.8.clone.1), dimensions={0}, to_apply=%region_1.2 | reduce | flops 1327104 | bytes 8847364 | tf_op jit(solution)/shard_map/reduce_sum | solution.py:66
  (9 shorter events, 0.1 us)
Async XLA Ops:
  7.2 35.6 %all-gather.4.cloned.1.call-start = ((), (), s32[]{:S(2)}) async-start(), calls=%async_computation.1 | async-start | bytes 4718592 | tf_op jit(solution)/shard_map/all_gather | solution.py:32
  9.4 2.2 copy-start.1
  11.7 14.1 %collective-permute-start.1 = (bf16[2,256,384]{2,1,0:T(8,128)(2,1)S(1)}, bf16[2,256,384]{2,1,0:T(8,128)(2,1)S(1)}, u32[]{:S(2)}, u32[]{:S(2)}) collective-permute-start(bf16[2,256,384]{2,1,0:T(8,128)(2,1)S(1)} %get-tuple-element.15), channel_id=1, source_target_pairs={{4,0},{8,4},{12,8},{5,1},{9,5},{13,9},{6,2},{10,6},{14,10},{7,3},{... | collective-permute-start | bytes 1179656 | tf_op jit(solution)/shard_map/ppermute | solution.py:10
  13.0 13.9 %collective-permute-start = (bf16[2,256,384]{2,1,0:T(8,128)(2,1)S(1)}, bf16[2,256,384]{2,1,0:T(8,128)(2,1)S(1)}, u32[]{:S(2)}, u32[]{:S(2)}) collective-permute-start(bf16[2,256,384]{2,1,0:T(8,128)(2,1)S(1)} %get-tuple-element.14), channel_id=1, source_target_pairs={{0,4},{4,8},{8,12},{1,5},{5,9},{9,13},{2,6},{6,10},{10,14},{3,7},{... | collective-permute-start | bytes 1179656 | tf_op jit(solution)/shard_map/ppermute | solution.py:10
  28.2 194.3 %all-gather.6.cloned.1.call-start = ((), (), s32[]{:S(2)}) async-start(), calls=%async_computation.2 | async-start | bytes 8847360 | tf_op jit(solution)/shard_map/all_gather | solution.py:66
  47.6 1.6 copy-start.2
  50.1 40.9 %collective-permute-start.2 = (f32[3,384,384]{2,1,0:T(8,128)S(1)}, f32[3,384,384]{2,1,0:T(8,128)S(1)}, u32[]{:S(2)}, u32[]{:S(2)}) collective-permute-start(f32[3,384,384]{2,1,0:T(8,128)S(1)} %fusion.38), channel_id=1, source_target_pairs={{0,2},{2,0},{1,3},{3,1},{4,6},{6,4},{5,7},{7,5},{8,10},{10,8},{9,1... | collective-permute-start | bytes 5308424 | tf_op jit(solution)/shard_map/ppermute | solution.py:62
  113.8 4.2 %copy-start = (bf16[512,3,768]{0,2,1:T(8,128)(2,1)S(1)}, bf16[512,3,768]{0,2,1:T(8,128)(2,1)}, u32[]{:S(2)}) copy-start(bf16[512,3,768]{0,2,1:T(8,128)(2,1)} %copy.20) | copy-start | bytes 7077892
Sparse Core Ops, SparseCore 0:
  28.4 14.3 all-gather.3
  93.1 129.3 all-gather.5
